TPU v7x, 256 devices: a whole 4x4x8 slice. The times are simulated.
256 devices in a mesh: req: 64 (over y_lo, z, x), tp: 4 (over y_hi, core).
Axes of the slice: x: 4, y: 4 (y_hi: 2, y_lo: 2; y = y_hi * 2 + y_lo), z: 8, core: 2. Of those that a mesh axis runs over, the one named last changes fastest.
Arguments:
- query_heads: bfloat16 [61440, 4096], P('req', 'tp'), parts along dimension 0, may hold values from -140 to 140
- normed_key_heads: bfloat16 [61440, 512], P('req', 'tp'), parts along dimension 0, may hold values from -7 to 7
- value_rows_per_head: bfloat16 [61440, 512], P('req', 'tp'), parts along dimension 0, may hold values from -6 to 6
- residual_in: bfloat16 [61440, 2048], P(('req', 'tp')), parts along dimension 0, may hold values from -6 to 6
- out_weight: bfloat16 [4096, 2048], P('tp'), may hold values from -0.09375 to 0.09375
- norm_gain: float32 [2048], replicated, may hold values from 0.3 to 3
- gate_up: bfloat16 [2, 2, 2048, 768], P(None, None, None, 'tp'), may hold values from -0.125 to 0.125
- down_weight: bfloat16 [2, 768, 2048], P(None, 'tp'), may hold values from -0.21875 to 0.21875
- segment_ids: int32 [61440], P('req'), parts along dimension 0, may hold values from 0 to 5, never falling along the last dimension, each value on 1 to 480 neighbouring positions
- expert_ids: int32 [61440, 8], P('req'), parts along dimension 0, may hold values from 0 to 127, all different within a row; in each aligned block of 960 rows (0 to 959, 960 to 1919, ...) at most 75 rows name the same one
- gate_weights: float32 [61440, 8], P('req'), parts along dimension 0, may hold values from 0.05 to 0.8
Outputs:
- layer_out: bfloat16 [61440, 2048], P(('req', 'tp')), parts along dimension 0
There are 64 independent parts, one for each index of `req`. A program takes and returns all parts, laid end to end along the dimension named above; an argument that names none is the same for every part. Nothing has to cross between parts.
Inputs may be any that keep to these rules, and one draw needn't show every extreme that they name: `segment_ids`: segment ids never fall along the tokens; each prompt has 1 to 480 tokens and one has exactly 480. `expert_ids`: the 8 experts of a token are distinct; no expert is chosen by more than 75 tokens of a request group, a bound that some block reaches.
All inputs are finite; a program needn't handle non-finite values.
Results may differ from a plain program's by a relative error of at most 0.0053.
Values may be sent and summed in bfloat16 or wider, within the bound.
No kernel may reach another device: no remote copies, remote signals or barrier semaphores. Data moves between devices by JAX's collectives and lax.ppermute only.
A program may use at most 128 MiB of HBM per device.

v0:
```python
import math

import jax
import jax.numpy as jnp
from jax import lax
from jax.sharding import PartitionSpec as P

QUERY_HEADS = 32
KEY_VALUE_HEADS = 4
HEAD_WIDTH = 128
EXPERTS = 128


def positions_of(segment_ids):
    earlier = (segment_ids[None, :] < segment_ids[:, None]).astype(jnp.int32)
    return jnp.arange(segment_ids.shape[0], dtype=jnp.int32) - jnp.sum(earlier, axis=1)


def rotary_tables(vectors, token_positions):
    half_dim = vectors.shape[-1] // 2
    frequency = 1000000.0 ** (-jnp.arange(half_dim, dtype=jnp.float32) / half_dim)
    angles = token_positions.astype(jnp.float32)[:, None] * frequency[None, :]
    cosine = jnp.cos(angles)[:, None, :]
    sine = jnp.sin(angles)[:, None, :]
    first = vectors[..., :half_dim]
    second = vectors[..., half_dim:]
    return jnp.concatenate(
        [first * cosine - second * sine, second * cosine + first * sine], axis=-1
    )


def rms_norm(hidden, gain):
    widened = hidden.astype(jnp.float32)
    factor = lax.rsqrt(jnp.mean(widened * widened, axis=-1, keepdims=True) + 1e-06)
    return (widened * factor * gain).astype(jnp.bfloat16)


def compact(chosen, limit):
    total = chosen.shape[0]
    iota = jnp.arange(total, dtype=jnp.int32)
    ranked = jnp.where(chosen, iota, iota + total)
    order = jnp.argsort(ranked, stable=True)[:limit]
    return (order, chosen[order])


def attend(query_heads, normed_key_heads, value_rows_per_head, segment_ids):
    item_count = segment_ids.shape[0]
    token_positions = positions_of(segment_ids)
    kv_local = normed_key_heads.shape[1] // HEAD_WIDTH
    query_group_width = QUERY_HEADS // KEY_VALUE_HEADS
    queries = rotary_tables(
        query_heads.reshape(item_count, kv_local * query_group_width, HEAD_WIDTH).astype(
            jnp.float32
        ),
        token_positions,
    ).astype(jnp.bfloat16)
    keys_after_rotary = rotary_tables(
        normed_key_heads.reshape(item_count, kv_local, HEAD_WIDTH).astype(jnp.float32),
        token_positions,
    ).astype(jnp.bfloat16)
    values = value_rows_per_head.reshape(item_count, kv_local, HEAD_WIDTH)
    indices = jnp.arange(item_count)
    allowed = (segment_ids[:, None] == segment_ids[None, :]) & (
        indices[None, :] <= indices[:, None]
    )
    factor = 1.0 / math.sqrt(HEAD_WIDTH)
    key_one = keys_after_rotary[:, 0]
    value_one = values[:, 0]

    def one_head(query_one, key_one=key_one, value_one=value_one):
        scores = jnp.dot(query_one, key_one.T, preferred_element_type=jnp.float32) * factor
        scores = jnp.where(allowed, scores, -1e30)
        peak = jnp.max(scores, axis=1, keepdims=True)
        weights = jnp.exp(scores - peak)
        weights = (weights / jnp.sum(weights, axis=1, keepdims=True)).astype(jnp.bfloat16)
        return jnp.dot(weights, value_one, preferred_element_type=jnp.float32).astype(jnp.bfloat16)

    group_queries = queries.transpose(1, 0, 2)
    blocks = lax.map(one_head, group_queries)
    attended = blocks.transpose(1, 0, 2)
    return attended.reshape(item_count, kv_local * query_group_width * HEAD_WIDTH)


def local(
    query_heads,
    normed_key_heads,
    value_rows_per_head,
    residual_in,
    out_weight,
    norm_gain,
    gate_up,
    down_weight,
    segment_ids,
    expert_ids,
    gate_weights,
):
    attended = attend(query_heads, normed_key_heads, value_rows_per_head, segment_ids)
    tok_rows = residual_in.shape[0]
    width = residual_in.shape[1]
    group_tokens = expert_ids.shape[0]
    capacity = group_tokens * expert_ids.shape[1] * 5 // (EXPERTS * 4)
    window = gate_up.shape[0]
    slots = jnp.arange(window, dtype=jnp.int32)
    route_all = jnp.sum(
        jnp.where(expert_ids[:, :, None] == slots[None, None, :], gate_weights[:, :, None], 0.0),
        axis=1,
    )
    normed_all = None
    rows = attended
    projected = lax.psum_scatter(
        jnp.dot(rows, out_weight, preferred_element_type=jnp.float32),
        "tp",
        scatter_dimension=0,
        tiled=True,
    )
    mixed = (residual_in.astype(jnp.float32) + projected).astype(jnp.bfloat16)
    normed = rms_norm(mixed, norm_gain)
    normed_all = lax.all_gather(normed, "tp", axis=0, tiled=True)
    rows = normed_all
    limit = min(capacity, tok_rows * lax.axis_size("tp"))
    summed = jnp.zeros((tok_rows * lax.axis_size("tp"), width), jnp.float32)
    for expert in range(window):
        taken, valid = compact(jnp.any(expert_ids == expert, axis=1), limit)
        picked = rows[taken]
        gate = jnp.dot(picked, gate_up[expert, 0], preferred_element_type=jnp.float32)
        upward = jnp.dot(picked, gate_up[expert, 1], preferred_element_type=jnp.float32)
        active = (jax.nn.silu(gate) * upward).astype(jnp.bfloat16)
        outputs = jnp.dot(active, down_weight[expert], preferred_element_type=jnp.float32)
        scale = jnp.where(valid, route_all[taken, expert], 0.0)
        summed = summed.at[taken].add(scale[:, None] * outputs)
    experts = lax.psum_scatter(summed, "tp", scatter_dimension=0, tiled=True)
    return (mixed.astype(jnp.float32) + experts).astype(jnp.bfloat16)


def solution(mesh):
    placed = (
        P("req", "tp"),
        P("req", "tp"),
        P("req", "tp"),
        P(("req", "tp"), None),
        P("tp", None),
        P(),
        P(None, None, None, "tp"),
        P(None, "tp", None),
        P("req"),
        P("req", None),
        P("req", None),
    )
    return jax.shard_map(
        local, mesh=mesh, in_specs=placed, out_specs=P(("req", "tp"), None), check_vma=False
    )
```

profile of v0, /device:TPU:1, one launch (start us, length us, event | category | flops | bytes accessed | tf_op | source)
XLA Modules:
  0.0 299.4 jit_solution(11987907407622865133)
XLA Ops:
  6.6 1.4 convert_reduce_fusion
  9.0 1.8 multiply_cosine_fusion.1
  10.7 2.3 fusion.49
  14.4 1.5 subtract_convert_fusion
  18.0 25.1 %while.11 = (s32[]{:T(128)}, bf16[8,960,128]{2,1,0:T(8,128)(2,1)}, bf16[8,960,128]{2,1,0:T(8,128)(2,1)S(1)}, bf16[960,128]{1,0:T(8,128)(2,1)S(1)}, bf16[960,128]...) while((s32[]{:T(128)}, bf16[8,960,128]{2,1,0:T(8,128)(2,1)}, ...), condition=%wide.region_4.5_spmd.clone, body=%wide.region_1.4_spmd.clone.sunk | while | flops 482117760 | bytes 12069725 | solution.py:79
  19.6 1.5 fusion.83
  22.7 1.5 fusion.83
  25.8 1.6 fusion.83
  29.0 1.6 fusion.83
  32.1 1.6 fusion.83
  35.3 1.6 fusion.83
  38.4 1.6 fusion.83
  41.6 1.5 fusion.83
  43.1 10.1 %fusion.17 = f32[960,2048]{1,0:T(8,128)} fusion(bf16[1024,2048]{1,0:T(8,128)(2,1)} %param.17, bf16[8,960,128]{2,1,0:T(8,128)(2,1)} %get-tuple-element.39), kind=kOutput, calls=%fused_computation.37 | convolution fusion | flops 4026531840 | bytes 14024704 | tf_op jit(solution)/shard_map/dot_general | solution.py:111
  53.5 85.1 %reduce-scatter.3.cloned.1.call-done = f32[240,2048]{1,0:T(8,128)} async-done(((f32[960,2048]{1,0:T(8,128)}), f32[240,2048]{1,0:T(8,128)}) %reduce-scatter.3.cloned.1.call-update) | async-done | bytes 1966096 | tf_op jit(solution)/shard_map/reduce_scatter | solution.py:110
  138.6 1.9 fusion.13
  141.9 4.4 %sort.32 = (s32[960]{0:T(1024)}, s32[960]{0:T(1024)S(1)}) sort(s32[960]{0:T(1024)S(1)} %get-tuple-element.103, s32[960]{0:T(1024)S(1)} %iota.47), dimensions={0}, to_apply=%region_12.13 | sort | flops 9600 | bytes 15360 | tf_op jit(solution)/shard_map/jit(argsort)/sort | solution.py:42
  146.3 1.3 gather_fusion.3
  147.6 2.0 gather_fusion.4
  149.7 4.4 %sort.31 = (s32[960]{0:T(1024)}, s32[960]{0:T(1024)S(1)}) sort(s32[960]{0:T(1024)S(1)} %get-tuple-element.104, s32[960]{0:T(1024)S(1)} %iota.45), dimensions={0}, to_apply=%region_7.8 | sort | flops 9600 | bytes 15360 | tf_op jit(solution)/shard_map/jit(argsort)/sort | solution.py:42
  154.0 2.0 gather_fusion.1
  157.4 24.6 %all-gather.2.cloned.1.call-done = bf16[960,2048]{1,0:T(8,128)(2,1)} async-done(((bf16[240,2048]{1,0:T(8,128)(2,1)}), bf16[960,2048]{1,0:T(8,128)(2,1)}) %all-gather.2.cloned.1.call-update) | async-done | bytes 3932176 | tf_op jit(solution)/shard_map/all_gather | solution.py:118
  182.0 3.7 %gather_fusion.2 = bf16[75,2048]{1,0:T(8,128)(2,1)S(1)} fusion(bf16[960,2048]{1,0:T(8,128)(2,1)} %all-gather.2.cloned.1.call-done, s32[1024]{0:T(1024)S(1)} %pad_clamp_fusion.1), kind=kCustom, calls=%fused_computation.2 | custom fusion | bytes 614700 | tf_op jit(solution)/shard_map/gather | solution.py:124
  185.7 1.5 fusion.30
  187.2 3.7 %gather_fusion.5 = bf16[75,2048]{1,0:T(8,128)(2,1)S(1)} fusion(bf16[960,2048]{1,0:T(8,128)(2,1)} %all-gather.2.cloned.1.call-done, s32[1024]{0:T(1024)S(1)} %pad_clamp_fusion), kind=kCustom, calls=%fused_computation.5 | custom fusion | bytes 614700 | tf_op jit(solution)/shard_map/gather | solution.py:124
  190.9 1.5 fusion.25
  192.4 2.1 convolution_multiply_fusion
  194.6 2.1 convolution_multiply_fusion.1
  196.7 5.0 %scatter_custom_fusion = f32[960,2048]{1,0:T(8,128)} fusion(s32[75]{0:T(128)S(1)} %get-tuple-element.92, f32[75,2048]{1,0:T(8,128)S(1)} %convolution_multiply_fusion.1, f32[]{:T(128)} %constant.16.clone.1), kind=kCustom, calls=%fused_computation.23 | custom fusion | flops 153600 | bytes 7864324 | tf_op jit(solution)/shard_map/scatter-add | solution.py:130
  201.8 7.8 %scatter_fusion = f32[960,2048]{1,0:T(8,128)} fusion(f32[960,2048]{1,0:T(8,128)} %scatter_custom_fusion, s32[75]{0:T(128)S(1)} %get-tuple-element.90, f32[75,2048]{1,0:T(8,128)S(1)} %convolution_multiply_fusion), kind=kCustom, calls=%fused_computation.7 | custom fusion | flops 153600 | bytes 1843500 | tf_op jit(solution)/shard_map/scatter-add | solution.py:130
  209.6 80.6 %reduce-scatter.5.cloned.1.call-done = f32[240,2048]{1,0:T(8,128)} async-done(((f32[960,2048]{1,0:T(8,128)}), f32[240,2048]{1,0:T(8,128)}) %reduce-scatter.5.cloned.1.call-update) | async-done | bytes 1966096 | tf_op jit(solution)/shard_map/reduce_scatter | solution.py:131
  290.1 2.7 fusion.16
  (59 shorter events, 20.0 us)
Async XLA Ops:
  6.5 6.5 %copy-start = (bf16[960,1024]{1,0:T(8,128)(2,1)S(1)}, bf16[960,1024]{1,0:T(8,128)(2,1)}, u32[]{:S(2)}) copy-start(bf16[960,1024]{1,0:T(8,128)(2,1)} %param.13) | copy-start | bytes 5898244
  6.5 132.1 %reduce-scatter.3.cloned.1.call-start = ((), (), s32[]{:S(2)}) async-start(), calls=%async_computation.2 | async-start | bytes 9830400 | tf_op jit(solution)/shard_map/reduce_scatter | solution.py:110
  17.0 0.7 copy-start.4
  17.0 1.0 copy-start.6
  53.2 85.4 %copy-start.1 = (bf16[240,2048]{1,0:T(8,128)(2,1)S(1)}, bf16[240,2048]{1,0:T(8,128)(2,1)}, u32[]{:S(2)}) copy-start(bf16[240,2048]{1,0:T(8,128)(2,1)} %param.16) | copy-start | bytes 2949124
  53.2 87.3 %copy-start.5 = (f32[2048]{0:T(1024)S(1)}, f32[2048]{0:T(1024)}, u32[]{:S(2)}) copy-start(f32[2048]{0:T(1024)} %param.18) | copy-start | bytes 24580
  53.2 88.6 %copy-start.2 = (s32[960,8]{0,1:T(8,128)S(1)}, s32[960,8]{0,1:T(8,128)}, u32[]{:S(2)}) copy-start(s32[960,8]{0,1:T(8,128)} %param.22) | copy-start | bytes 92164
  53.3 94.3 %copy-start.3 = (f32[960,8]{0,1:T(8,128)S(1)}, f32[960,8]{0,1:T(8,128)}, u32[]{:S(2)}) copy-start(f32[960,8]{0,1:T(8,128)} %param.23) | copy-start | bytes 92164
  53.3 128.8 %all-gather.2.cloned.1.call-start = ((), (), s32[]{:S(2)}) async-start(), calls=%async_computation.3 | async-start | bytes 4915200 | tf_op jit(solution)/shard_map/all_gather | solution.py:118
  141.8 148.3 %reduce-scatter.5.cloned.1.call-start = ((), (), s32[]{:S(2)}) async-start(), calls=%async_computation.4 | async-start | bytes 9830400 | tf_op jit(solution)/shard_map/reduce_scatter | solution.py:131
Sparse Core Ops, SparseCore 0:
  53.4 85.1 reduce-scatter.2
  141.9 40.0 all-gather.1
  209.7 80.3 reduce-scatter.4
where the time goes:
time: 300 us; the launch traced here: 299 us
  waiting for transfers between devices  190 us (63%)
  other arithmetic  41.9 us (14%)
  matrix products  37.7 us (13%)
  local copies, waits for them, and re-layouts  15.8 us (5%)
  between operations  13.4 us (4%)
    reduce_scatter x1, waiting for transfers between devices, local(): lax.psum_scatter(jnp.dot(rows, out_weight, preferred_element_type=jnp.flo...  85.1 us
    reduce_scatter x1, waiting for transfers between devices, local(): experts = lax.psum_scatter(summed, 'tp', scatter_dimension=0, tiled=True)  80.6 us
    all_gather x1, waiting for transfers between devices, local(): normed_all = lax.all_gather(normed, 'tp', axis=0, tiled=True)  24.6 us
    scatter-add x2, other arithmetic, local(): summed = summed.at[taken].add(scale[:, None] * outputs)  12.8 us
    dot_general x8, matrix products, one_head(): jnp.dot(weights, value_one, preferred_element_type=jnp.float32)  12.4 us
    dot_general x1, matrix products, local(): jnp.dot(rows, out_weight, preferred_element_type=jnp.float32)  10.1 us
    sort x2, other arithmetic, compact(): order = jnp.argsort(ranked, stable=True)[:limit]  8.71 us
    dot_general x8, matrix products, one_head(): jnp.dot(query_one, key_one.T, preferred_element_type=jnp.float32) * factor  7.91 us
  transfers between devices with their start and end apart: 3, of which 3 were waited for; matrix products, arithmetic and copies ran while one was open for 5% of the time, Pallas kernels for 0%

commit v1 on v0

--- a/solution.py
+++ b/solution.py
@@ -33,14 +33,6 @@
     widened = hidden.astype(jnp.float32)
     factor = lax.rsqrt(jnp.mean(widened * widened, axis=-1, keepdims=True) + 1e-06)
     return (widened * factor * gain).astype(jnp.bfloat16)
-
-
-def compact(chosen, limit):
-    total = chosen.shape[0]
-    iota = jnp.arange(total, dtype=jnp.int32)
-    ranked = jnp.where(chosen, iota, iota + total)
-    order = jnp.argsort(ranked, stable=True)[:limit]
-    return (order, chosen[order])
 
 
 def attend(query_heads, normed_key_heads, value_rows_per_head, segment_ids):
@@ -96,39 +88,41 @@
 ):
     attended = attend(query_heads, normed_key_heads, value_rows_per_head, segment_ids)
     tok_rows = residual_in.shape[0]
-    width = residual_in.shape[1]
     group_tokens = expert_ids.shape[0]
-    capacity = group_tokens * expert_ids.shape[1] * 5 // (EXPERTS * 4)
+    capacity = min(group_tokens * expert_ids.shape[1] * 5 // (EXPERTS * 4), group_tokens)
     window = gate_up.shape[0]
     slots = jnp.arange(window, dtype=jnp.int32)
-    route_all = jnp.sum(
-        jnp.where(expert_ids[:, :, None] == slots[None, None, :], gate_weights[:, :, None], 0.0),
-        axis=1,
+    hits = expert_ids[:, :, None] == slots[None, None, :]
+    route_all = jnp.sum(jnp.where(hits, gate_weights[:, :, None], 0.0), axis=1)
+    chosen = jnp.any(hits, axis=1)
+    rank = jnp.cumsum(chosen.astype(jnp.int32), axis=0) - 1
+    kk = jnp.arange(capacity, dtype=jnp.int32)
+    select_all = (rank.T[:, None, :] == kk[None, :, None]) & chosen.T[:, None, :]
+    route_sel = jnp.sum(jnp.where(select_all, route_all.T[:, None, :], 0.0), axis=-1)
+    first = lax.axis_index("tp") * tok_rows
+    select_loc = lax.dynamic_slice_in_dim(select_all, first, tok_rows, axis=2)
+
+    partial = jnp.dot(attended, out_weight, preferred_element_type=jnp.float32)
+    projected = lax.psum_scatter(
+        partial.astype(jnp.bfloat16), "tp", scatter_dimension=0, tiled=True
     )
-    normed_all = None
-    rows = attended
-    projected = lax.psum_scatter(
-        jnp.dot(rows, out_weight, preferred_element_type=jnp.float32),
-        "tp",
-        scatter_dimension=0,
-        tiled=True,
+    mixed = (residual_in.astype(jnp.float32) + projected.astype(jnp.float32)).astype(jnp.bfloat16)
+    normed = rms_norm(mixed, norm_gain)
+
+    picked_own = jnp.einsum(
+        "ekt,td->ekd", select_loc.astype(jnp.bfloat16), normed,
+        preferred_element_type=jnp.float32,
+    ).astype(jnp.bfloat16)
+    picked = lax.psum(picked_own, "tp")
+    gate = jnp.einsum("ekd,edf->ekf", picked, gate_up[:, 0], preferred_element_type=jnp.float32)
+    upward = jnp.einsum("ekd,edf->ekf", picked, gate_up[:, 1], preferred_element_type=jnp.float32)
+    active = (jax.nn.silu(gate) * upward).astype(jnp.bfloat16)
+    outputs = jnp.einsum("ekf,efd->ekd", active, down_weight, preferred_element_type=jnp.float32)
+    scaled = lax.psum(route_sel[:, :, None] * outputs, "tp")
+    experts = jnp.einsum(
+        "ekt,ekd->td", select_loc.astype(jnp.float32), scaled,
+        precision=lax.Precision.HIGHEST, preferred_element_type=jnp.float32,
     )
-    mixed = (residual_in.astype(jnp.float32) + projected).astype(jnp.bfloat16)
-    normed = rms_norm(mixed, norm_gain)
-    normed_all = lax.all_gather(normed, "tp", axis=0, tiled=True)
-    rows = normed_all
-    limit = min(capacity, tok_rows * lax.axis_size("tp"))
-    summed = jnp.zeros((tok_rows * lax.axis_size("tp"), width), jnp.float32)
-    for expert in range(window):
-        taken, valid = compact(jnp.any(expert_ids == expert, axis=1), limit)
-        picked = rows[taken]
-        gate = jnp.dot(picked, gate_up[expert, 0], preferred_element_type=jnp.float32)
-        upward = jnp.dot(picked, gate_up[expert, 1], preferred_element_type=jnp.float32)
-        active = (jax.nn.silu(gate) * upward).astype(jnp.bfloat16)
-        outputs = jnp.dot(active, down_weight[expert], preferred_element_type=jnp.float32)
-        scale = jnp.where(valid, route_all[taken, expert], 0.0)
-        summed = summed.at[taken].add(scale[:, None] * outputs)
-    experts = lax.psum_scatter(summed, "tp", scatter_dimension=0, tiled=True)
     return (mixed.astype(jnp.float32) + experts).astype(jnp.bfloat16)
 
 

time: 300 us -> 246 us (0.82)
  waiting for transfers between devices: 190 us -> 156 us
  other arithmetic: 41.9 us -> 21.8 us
  matrix products: 37.7 us -> 48.4 us
  local copies, waits for them, and re-layouts: 15.8 us -> 5.37 us
    reduce_scatter x2 -> x1, waiting for transfers between devices: 166 us -> 56.1 us  [local(): lax.psum_scatter(partial.astype(jnp.bfloat16), 'tp', scatter_dimension=0,...]
    psum x0 -> x2, waiting for transfers between devices: none -> 99.5 us  [the longest x1 52.2 us: local(): scaled = lax.psum(route_sel[:, :, None] * outputs, 'tp')]
    all_gather x1 -> x0, waiting for transfers between devices: 24.6 us -> none  [local(): normed_all = lax.all_gather(normed, 'tp', axis=0, tiled=True)]
    gather x6 -> x0, local copies, waits for them, and re-layouts: 14 us -> none  [the longest x2 7.37 us: local(): picked = rows[taken]]
    scatter-add x2 -> x0, other arithmetic: 12.8 us -> none  [local(): summed = summed.at[taken].add(scale[:, None] * outputs)]
    sort x2 -> x0, other arithmetic: 8.71 us -> none  [compact(): order = jnp.argsort(ranked, stable=True)[:limit]]
    dot_general x8, matrix products: 7.91 us -> 14.7 us  [one_head(): jnp.dot(query_one, key_one.T, preferred_element_type=jnp.float32) * factor]
    convert_element_type x2 -> x0, other arithmetic: 3.98 us -> none  [the longest x1 2.75 us: local(): return (mixed.astype(jnp.float32) + experts).astype(jnp.bfloat16)]
  transfers between devices with their start and end apart: 3 -> 3, of which waited for: 3 -> 3; matrix products, arithmetic and copies ran while one was open for 5% -> 1% of each run, Pallas kernels for 0% -> 0%
where the time goes in v1:
time: 246 us; the launch traced here: 245 us
  waiting for transfers between devices  156 us (63%)
  matrix products  48.4 us (20%)
  other arithmetic  21.8 us (9%)
  between operations  13.2 us (5%)
  local copies, waits for them, and re-layouts  5.37 us (2%)
    reduce_scatter x1, waiting for transfers between devices, local(): lax.psum_scatter(partial.astype(jnp.bfloat16), 'tp', scatter_dimension=0,...  56.1 us
    psum x1, waiting for transfers between devices, local(): scaled = lax.psum(route_sel[:, :, None] * outputs, 'tp')  52.2 us
    psum x1, waiting for transfers between devices, local(): picked = lax.psum(picked_own, 'tp')  47.4 us
    dot_general x8, matrix products, one_head(): jnp.dot(query_one, key_one.T, preferred_element_type=jnp.float32) * factor  14.7 us
    dot_general x8, matrix products, one_head(): jnp.dot(weights, value_one, preferred_element_type=jnp.float32)  12.4 us
    dot_general x1, matrix products, local(): partial = jnp.dot(attended, out_weight, preferred_element_type=jnp.float32)  8.89 us
  transfers between devices with their start and end apart: 3, of which 3 were waited for; matrix products, arithmetic and copies ran while one was open for 1% of the time, Pallas kernels for 0%

profile of v1, /device:TPU:1, one launch (start us, length us, event | category | flops | bytes accessed | tf_op | source)
XLA Modules:
  0.0 244.8 jit_solution(6634711606771478389)
XLA Ops:
  6.6 1.4 convert_reduce_fusion
  8.0 2.0 convert_bitcast_fusion
  10.9 1.8 multiply_cosine_fusion.1
  12.7 1.5 subtract_convert_fusion
  16.2 3.0 %fusion.45 = (bf16[960,64]{1,0:T(8,128)(2,1)}, bf16[960,64]{1,0:T(8,128)(2,1)}) fusion(f32[960,1,128]{2,0,1:T(8,128)S(1)} %bitcast_convert_fusion, f32[64]{0:T(128)S(1)} %multiply_power_fusion, f32[960]{0:T(1024)S(1)} %subtract_convert_fusion.1), kind=kLoop, calls=%fused_computation.62 | loop fusion | flops 552960 | bytes 741376 | tf_op jit(solution)/shard_map/concatenate | solution.py:27
  19.2 1.9 pad_maximum_fusion
  21.1 34.7 %while.11 = (s32[]{:T(128)}, bf16[8,960,128]{2,1,0:T(8,128)(2,1)}, bf16[8,960,128]{2,1,0:T(8,128)(2,1)S(1)}, bf16[960,128]{1,0:T(8,128)(2,1)}, bf16[960,128]{1,0:T(8,128)(2,1)}, /*index=5*/s32[960]{0:T(1024)S(1)}, s32[]{:T(128)}) while((s32[]{:T(128)}, bf16[8,960,128]{2,1,0:T(8,128)(2,1)}, bf16[8,960,128]{2,1,0:T(8,128)(2,1)S(1)}, ...), condition=%wide.region_4.5_spmd.clone, body=%wide.region_1.4_spmd.clone.sunk | while | flops 482117760 | bytes 13053293 | solution.py:71
  21.1 1.8 fusion.76
  23.9 1.6 fusion.78
  25.5 1.8 fusion.76
  28.2 1.5 fusion.78
  29.8 1.8 fusion.76
  32.5 1.5 fusion.78
  34.1 1.8 fusion.76
  36.9 1.6 fusion.78
  38.4 1.8 fusion.76
  41.2 1.6 fusion.78
  42.8 1.8 fusion.76
  45.6 1.5 fusion.78
  47.1 1.8 fusion.76
  49.9 1.6 fusion.78
  51.4 1.8 fusion.76
  54.2 1.5 fusion.78
  55.8 8.9 %convolution_convert_fusion = bf16[960,2048]{1,0:T(8,128)(2,1)} fusion(bf16[1024,2048]{1,0:T(8,128)(2,1)} %param.17, bf16[8,960,128]{2,1,0:T(8,128)(2,1)} %get-tuple-element.37), kind=kOutput, calls=%fused_computation.18 | convolution fusion | flops 4028497920 | bytes 10092544 | tf_op jit(solution)/shard_map/dot_general | solution.py:105
  67.3 56.1 %reduce-scatter.2.cloned.1.call-done = bf16[240,2048]{1,0:T(8,128)(2,1)} async-done(((bf16[960,2048]{1,0:T(8,128)(2,1)}), bf16[240,2048]{1,0:T(8,128)(2,1)}) %reduce-scatter.2.cloned.1.call-update) | async-done | bytes 983056 | tf_op jit(solution)/shard_map/reduce_scatter | solution.py:106
  123.5 1.7 fusion.12
  125.2 2.3 convolution_convert_fusion.1
  128.5 47.4 %all-reduce.4.cloned.1.call-done = bf16[2,75,2048]{2,1,0:T(8,128)(2,1)} async-done(((bf16[2,75,2048]{2,1,0:T(8,128)(2,1)}), bf16[2,75,2048]{2,1,0:T(8,128)(2,1)}) %all-reduce.4.cloned.1.call-update) | async-done | bytes 614416 | tf_op jit(solution)/shard_map/psum | solution.py:116
  175.9 2.9 %fusion.19 = f32[2,75,192]{2,1,0:T(8,128)} fusion(bf16[2,75,2048]{2,1,0:T(8,128)(2,1)} %all-reduce.4.cloned.1.call-done, bf16[2,2,2048,192]{2,3,1,0:T(8,128)(2,1)} %param.19), kind=kOutput, calls=%fused_computation.35 | convolution fusion | flops 117964800 | bytes 2343424 | tf_op jit(solution)/shard_map/ekd,edf->ekf/dot_general | solution.py:117
  178.8 3.7 %convolution_multiply_fusion = f32[2,75,2048]{2,1,0:T(8,128)} fusion(bf16[2,192,2048]{2,1,0:T(8,128)(2,1)S(1)} %copy-done, bf16[2,75,2048]{2,1,0:T(8,128)(2,1)} %all-reduce.4.cloned.1.call-done, bf16[2,2,2048,192]{2,3,1,0:T(8,128)(2,1)} %param.19, f32[2,75]{1,0:T(2,128)S(1)} %select_reduce_fusion, f32[2,75,192]{2,1,0:T(8,128)} %fusion.19), kind=kOutput, calls=%fused_computation.24 | convolution fusion | flops 236409600 | bytes 5194328 | tf_op jit(solution)/shard_map/ekf,efd->ekd/dot_general | solution.py:120
  182.5 52.2 %all-reduce.6.cloned.1.call-done = f32[2,75,2048]{2,1,0:T(8,128)} async-done(((f32[2,75,2048]{2,1,0:T(8,128)}), f32[2,75,2048]{2,1,0:T(8,128)}) %all-reduce.6.cloned.1.call-update) | async-done | bytes 1228816 | tf_op jit(solution)/shard_map/psum | solution.py:121
  234.7 3.6 %fusion.11 = bf16[240,2048]{1,0:T(8,128)(2,1)} fusion(f32[2,75,2048]{2,1,0:T(8,128)} %all-reduce.6.cloned.1.call-done, pred[2,75,960]{2,1,0:T(8,128)(4,1)} %fusion.39, s32[]{:T(128)S(6)} %select_n.15, bf16[240,2048]{1,0:T(8,128)(2,1)S(1)} %copy-done.2, bf16[240,2048]{1,0:T(8,128)(2,1)S(1)} %copy-done.1), kind=kOutput, calls=%fused_computation.23 | convolution fusion | flops 888176640 | bytes 4300804 | tf_op jit(solution)/shard_map/ekt,ekd->td/dot_general | solution.py:122
  (62 shorter events, 14.3 us)
Async XLA Ops:
  6.5 172.3 %copy-start = (bf16[2,192,2048]{2,1,0:T(8,128)(2,1)S(1)}, bf16[2,192,2048]{2,1,0:T(8,128)(2,1)}, u32[]{:S(2)}) copy-start(bf16[2,192,2048]{2,1,0:T(8,128)(2,1)} %param.20) | copy-start | bytes 4718596
  6.5 116.9 %reduce-scatter.2.cloned.1.call-start = ((), (), s32[]{:S(2)}) async-start(), calls=%async_computation.1 | async-start | bytes 4915200 | tf_op jit(solution)/shard_map/reduce_scatter | solution.py:106
  15.2 0.9 copy-start.3
  16.2 4.9 %copy-start.5 = (s32[960]{0:T(1024)S(1)}, s32[960]{0:T(1024)}, u32[]{:S(2)}) copy-start(s32[960]{0:T(1024)} %param.21) | copy-start | bytes 11524
  22.9 0.9 copy-start.6
  27.3 0.9 copy-start.6
  31.6 0.9 copy-start.6
  35.9 0.9 copy-start.6
  40.3 0.9 copy-start.6
  44.6 0.9 copy-start.6
  48.9 0.9 copy-start.6
  53.3 0.9 copy-start.6
  64.7 0.8 copy-start.4
  64.7 58.8 %copy-start.1 = (bf16[240,2048]{1,0:T(8,128)(2,1)S(1)}, bf16[240,2048]{1,0:T(8,128)(2,1)}, u32[]{:S(2)}) copy-start(bf16[240,2048]{1,0:T(8,128)(2,1)} %param.16) | copy-start | bytes 2949124
  64.7 111.2 %all-reduce.4.cloned.1.call-start = ((), (), s32[]{:S(2)}) async-start(), calls=%async_computation.2 | async-start | bytes 1310720 | tf_op jit(solution)/shard_map/psum | solution.py:116
  123.5 1.7 copy-start.2
  127.5 107.3 %all-reduce.6.cloned.1.call-start = ((), (), s32[]{:S(2)}) async-start(), calls=%async_computation.3 | async-start | bytes 2621440 | tf_op jit(solution)/shard_map/psum | solution.py:121
Sparse Core Ops, SparseCore 0:
  64.8 58.5 reduce-scatter.1
  127.6 48.2 all-reduce.3
  182.7 52.0 all-reduce.5

commit v2 on v1

v2 whole, which is shorter than its diff:
```python
import math

import jax
import jax.numpy as jnp
from jax import lax
from jax.sharding import PartitionSpec as P

QUERY_HEADS = 32
KEY_VALUE_HEADS = 4
HEAD_WIDTH = 128
EXPERTS = 128


def positions_of(segment_ids):
    earlier = (segment_ids[None, :] < segment_ids[:, None]).astype(jnp.int32)
    return jnp.arange(segment_ids.shape[0], dtype=jnp.int32) - jnp.sum(earlier, axis=1)


def rotary_tables(vectors, token_positions):
    half_dim = vectors.shape[-1] // 2
    frequency = 1000000.0 ** (-jnp.arange(half_dim, dtype=jnp.float32) / half_dim)
    angles = token_positions.astype(jnp.float32)[:, None] * frequency[None, :]
    cosine = jnp.cos(angles)[:, None, :]
    sine = jnp.sin(angles)[:, None, :]
    first = vectors[..., :half_dim]
    second = vectors[..., half_dim:]
    return jnp.concatenate(
        [first * cosine - second * sine, second * cosine + first * sine], axis=-1
    )


def rms_norm(hidden, gain):
    widened = hidden.astype(jnp.float32)
    factor = lax.rsqrt(jnp.mean(widened * widened, axis=-1, keepdims=True) + 1e-06)
    return (widened * factor * gain).astype(jnp.bfloat16)


SEG_MOST = 480


def xor_pairs(size, mask):
    return [(index, index ^ mask) for index in range(size)]


def attend_block(query_rows, first, keys_after_rotary, values, segment_ids, token_positions):
    rows = query_rows.shape[0]
    item_count = segment_ids.shape[0]
    span = min(item_count, rows + SEG_MOST)
    head_count = query_rows.shape[1] // HEAD_WIDTH
    start = jnp.clip(first + rows - span, 0, item_count - span)
    row_index = first + jnp.arange(rows, dtype=jnp.int32)
    key_index = start + jnp.arange(span, dtype=jnp.int32)
    row_segment = lax.dynamic_slice_in_dim(segment_ids, first, rows)
    key_segment = lax.dynamic_slice_in_dim(segment_ids, start, span)
    allowed = (row_segment[:, None] == key_segment[None, :]) & (
        key_index[None, :] <= row_index[:, None]
    )
    key_one = lax.dynamic_slice_in_dim(keys_after_rotary, start, span)
    value_one = lax.dynamic_slice_in_dim(values, start, span)
    queries = rotary_tables(
        query_rows.reshape(rows, head_count, HEAD_WIDTH).astype(jnp.float32),
        lax.dynamic_slice_in_dim(token_positions, first, rows),
    ).astype(jnp.bfloat16)
    factor = 1.0 / math.sqrt(HEAD_WIDTH)

    def one_head(query_one):
        scores = jnp.dot(query_one, key_one.T, preferred_element_type=jnp.float32) * factor
        scores = jnp.where(allowed, scores, -1e30)
        peak = jnp.max(scores, axis=1, keepdims=True)
        weights = jnp.exp(scores - peak)
        weights = (weights / jnp.sum(weights, axis=1, keepdims=True)).astype(jnp.bfloat16)
        return jnp.dot(weights, value_one, preferred_element_type=jnp.float32).astype(jnp.bfloat16)

    blocks = lax.map(one_head, queries.transpose(1, 0, 2))
    return blocks.transpose(1, 0, 2).reshape(rows, head_count * HEAD_WIDTH)


def local(
    query_heads,
    normed_key_heads,
    value_rows_per_head,
    residual_in,
    out_weight,
    norm_gain,
    gate_up,
    down_weight,
    segment_ids,
    expert_ids,
    gate_weights,
):
    tok_rows = residual_in.shape[0]
    group_tokens = expert_ids.shape[0]
    size = lax.axis_size("tp")
    me = lax.axis_index("tp")
    token_positions = positions_of(segment_ids)
    keys_after_rotary = rotary_tables(
        normed_key_heads.reshape(group_tokens, 1, HEAD_WIDTH).astype(jnp.float32), token_positions
    ).astype(jnp.bfloat16)[:, 0]
    values = value_rows_per_head

    def projected_block(block):
        first = block * tok_rows
        query_rows = lax.dynamic_slice_in_dim(query_heads, first, tok_rows)
        attended = attend_block(
            query_rows, first, keys_after_rotary, values, segment_ids, token_positions
        )
        return jnp.dot(attended, out_weight, preferred_element_type=jnp.float32)

    to_partner = jnp.stack([projected_block(me ^ 1), projected_block(me ^ 3)]).astype(jnp.bfloat16)
    from_partner = lax.ppermute(to_partner, "tp", xor_pairs(size, 1))
    across = projected_block(me ^ 2) + from_partner[1].astype(jnp.float32)
    from_across = lax.ppermute(across.astype(jnp.bfloat16), "tp", xor_pairs(size, 2))
    projected = (
        projected_block(me)
        + from_partner[0].astype(jnp.float32)
        + from_across.astype(jnp.float32)
    )
    mixed = (residual_in.astype(jnp.float32) + projected).astype(jnp.bfloat16)
    normed = rms_norm(mixed, norm_gain)

    capacity = min(group_tokens * expert_ids.shape[1] * 5 // (EXPERTS * 4), group_tokens)
    window = gate_up.shape[0]
    slots = jnp.arange(window, dtype=jnp.int32)
    hits = expert_ids[:, :, None] == slots[None, None, :]
    route_all = jnp.sum(jnp.where(hits, gate_weights[:, :, None], 0.0), axis=1)
    chosen = jnp.any(hits, axis=1)
    rank = jnp.cumsum(chosen.astype(jnp.int32), axis=0) - 1
    kk = jnp.arange(capacity, dtype=jnp.int32)
    select_all = (rank.T[:, None, :] == kk[None, :, None]) & chosen.T[:, None, :]
    route_sel = jnp.sum(jnp.where(select_all, route_all.T[:, None, :], 0.0), axis=-1)
    select_loc = lax.dynamic_slice_in_dim(select_all, me * tok_rows, tok_rows, axis=2)

    picked = jnp.einsum(
        "ekt,td->ekd", select_loc.astype(jnp.bfloat16), normed,
        preferred_element_type=jnp.float32,
    ).astype(jnp.bfloat16)
    picked = picked + lax.ppermute(picked, "tp", xor_pairs(size, 1))
    picked = picked + lax.ppermute(picked, "tp", xor_pairs(size, 2))
    gate = jnp.einsum("ekd,edf->ekf", picked, gate_up[:, 0], preferred_element_type=jnp.float32)
    upward = jnp.einsum("ekd,edf->ekf", picked, gate_up[:, 1], preferred_element_type=jnp.float32)
    active = (jax.nn.silu(gate) * upward).astype(jnp.bfloat16)
    outputs = jnp.einsum("ekf,efd->ekd", active, down_weight, preferred_element_type=jnp.float32)
    scaled = route_sel[:, :, None] * outputs
    scaled = scaled + lax.ppermute(scaled, "tp", xor_pairs(size, 1))
    scaled = scaled + lax.ppermute(
        scaled.astype(jnp.bfloat16), "tp", xor_pairs(size, 2)
    ).astype(jnp.float32)
    experts = jnp.einsum(
        "ekt,ekd->td", select_loc.astype(jnp.float32), scaled,
        precision=lax.Precision.HIGHEST, preferred_element_type=jnp.float32,
    )
    return (mixed.astype(jnp.float32) + experts).astype(jnp.bfloat16)


def solution(mesh):
    placed = (
        P("req", "tp"),
        P("req", "tp"),
        P("req", "tp"),
        P(("req", "tp"), None),
        P("tp", None),
        P(),
        P(None, None, None, "tp"),
        P(None, "tp", None),
        P("req"),
        P("req", None),
        P("req", None),
    )
    return jax.shard_map(
        local, mesh=mesh, in_specs=placed, out_specs=P(("req", "tp"), None), check_vma=False
    )
```

time: 246 us -> 205 us (0.83)
  waiting for transfers between devices: 156 us -> 56.7 us
  matrix products: 48.4 us -> 82.5 us
  local copies, waits for them, and re-layouts: 5.37 us -> 21.7 us
  between operations: 13.2 us -> 0.64 us
  other arithmetic: 21.8 us -> 32.5 us
  starting transfers between devices: 0.27 us -> 9.56 us
    psum x2 -> x0, waiting for transfers between devices: 99.5 us -> none  [the longest x1 52.2 us: local(): scaled = lax.psum(route_sel[:, :, None] * outputs, 'tp')]
    ppermute x0 -> x6, waiting for transfers between devices: none -> 56.7 us  [the longest x1 22.1 us: local(): lax.ppermute(across.astype(jnp.bfloat16), 'tp', xor_pairs(size, 2))]
    reduce_scatter x1 -> x0, waiting for transfers between devices: 56.1 us -> none  [local(): lax.psum_scatter(partial.astype(jnp.bfloat16), 'tp', scatter_dimension=0,...]
    dot_general x8 -> x32, matrix products: 14.7 us -> 35.3 us  [one_head(): jnp.dot(query_one, key_one.T, preferred_element_type=jnp.float32) * factor]
    dot_general x8 -> x32, matrix products: 12.4 us -> 27.5 us  [one_head(): jnp.dot(weights, value_one, preferred_element_type=jnp.float32)]
    ppermute x0 -> x6, starting transfers between devices: none -> 9.56 us  [the longest x1 3.21 us: local(): from_partner = lax.ppermute(to_partner, 'tp', xor_pairs(size, 1))]
    unnamed x16 -> x89, local copies, waits for them, and re-layouts: 2.4 us -> 9.19 us
    dynamic_slice x0 -> x5, local copies, waits for them, and re-layouts: none -> 6.69 us  [the longest x4 4.46 us: attend_block(): key_one = lax.dynamic_slice_in_dim(keys_after_rotary, start, span)]
  transfers between devices with their start and end apart: 3 -> 6, of which waited for: 3 -> 5; matrix products, arithmetic and copies ran while one was open for 1% -> 18% of each run, Pallas kernels for 0% -> 0%
where the time goes in v2:
time: 205 us; the launch traced here: 204 us
  matrix products  82.5 us (40%)
  waiting for transfers between devices  56.7 us (28%)
  other arithmetic  32.5 us (16%)
  local copies, waits for them, and re-layouts  21.7 us (11%)
  starting transfers between devices  9.56 us (5%)
    dot_general x32, matrix products, one_head(): jnp.dot(query_one, key_one.T, preferred_element_type=jnp.float32) * factor  35.3 us
    dot_general x32, matrix products, one_head(): jnp.dot(weights, value_one, preferred_element_type=jnp.float32)  27.5 us
    ppermute x1, waiting for transfers between devices, local(): lax.ppermute(across.astype(jnp.bfloat16), 'tp', xor_pairs(size, 2))  22.1 us
    ppermute x1, waiting for transfers between devices, local(): lax.ppermute(scaled.astype(jnp.bfloat16), 'tp', xor_pairs(size, 2))  15.3 us
    ppermute x1, waiting for transfers between devices, local(): picked = picked + lax.ppermute(picked, 'tp', xor_pairs(size, 2))  15.1 us
    dot_general x4, matrix products, projected_block(): return jnp.dot(attended, out_weight, preferred_element_type=jnp.float32)  11.1 us
    unnamed x89, local copies, waits for them, and re-layouts  9.19 us
    reduce_sum x32, other arithmetic, one_head(): jnp.sum(weights, axis=1, keepdims=True)  8.45 us
  transfers between devices with their start and end apart: 6, of which 5 were waited for; matrix products, arithmetic and copies ran while one was open for 18% of the time, Pallas kernels for 0%

profile of v2, /device:TPU:1, one launch (start us, length us, event | category | flops | bytes accessed | tf_op | source)
XLA Modules:
  0.0 204.0 jit_solution(8967127558445912724)
XLA Ops:
  3.1 1.5 dynamic-slice_convert_fusion.3
  4.6 3.2 %convert_bitcast_fusion.3 = (f32[30,8,8,128]{3,1,2,0:T(8,128)S(1)}, f32[30,8,8,128]{3,1,2,0:T(8,128)}, f32[30,8,8,128]{3,1,2,0:T(8,128)S(1)}, f32[30,8,8,128]{3,1,2,0:T(8,128)}) fusion(bf16[960,1024]{1,0:T(8,128)(2,1)} %param.19, s32[]{:T(128)S(6)} %select_n.28, s32[]{:T(128)S(6)} %select_n.30, s32[]{:T(128)S(6)} %select_n.57, s32[]{:T(128)S(6)} %select_n.56), kind=kLoop, calls=%fused_computation.85 | loop fusion | flops 983040 | bytes 5898256
  7.8 1.8 copy.83
  12.0 2.2 %constant_dynamic-slice_fusion.3 = (bf16[720,128]{1,0:T(8,128)(2,1)}, bf16[720,128]{1,0:T(8,128)(2,1)}, bf16[720,128]{1,0:T(8,128)(2,1)}, bf16[720,128]{1,0:T(8,128)(2,1)}) fusion(bf16[960,128]{1,0:T(8,128)(2,1)} %param.21, s32[]{:T(128)S(6)} %min.13, s32[]{:T(128)S(6)} %min.14, s32[]{:T(128)S(6)} %min.16, s32[]{:T(128)S(6)} %min.15), kind=kLoop, calls=%fused_computation.168 | loop fusion | bytes 1474576 | tf_op jit(solution)/shard_map/dynamic_slice | solution.py:59
  14.4 2.5 %multiply_cosine_fusion.4 = (f32[240,64]{1,0:T(8,128)}, f32[240,64]{1,0:T(8,128)}, f32[240,64]{1,0:T(8,128)S(1)}, f32[240,64]{1,0:T(8,128)S(1)}, f32[240,64]{1,0...) fusion(f32[64]{0:T(128)S(1)} %copy-done.34, f32[240]{0:T(256)S(1)} %get-tuple-element.525, ...), kind=kLoop, calls=%fused_computation.147 | loop fusion | flops 61440 | bytes 495616 | tf_op jit(solution)/shard_map/cos | solution.py:23
  19.7 1.4 fusion.82
  21.1 1.7 copy.87
  23.7 21.0 %while.45 = (s32[]{:T(128)}, bf16[8,240,128]{2,1,0:T(8,128)(2,1)}, bf16[8,240,128]{2,1,0:T(8,128)(2,1)}, bf16[720,128]{1,0:T(8,128)(2,1)}, bf16[720,128]{1,0:T(8...) while((s32[]{:T(128)}, bf16[8,240,128]{2,1,0:T(8,128)(2,1)}, ...), condition=%wide.region_8.9_spmd.clone, body=%wide.region_5.8_spmd.clone.sunk | while | flops 90404640 | bytes 3316097 | solution.py:74
  44.8 1.4 copy.114
  47.9 1.7 copy.90
  50.5 21.3 %while.46 = (s32[]{:T(128)}, bf16[8,240,128]{2,1,0:T(8,128)(2,1)}, bf16[8,240,128]{2,1,0:T(8,128)(2,1)}, bf16[720,128]{1,0:T(8,128)(2,1)}, bf16[720,128]{1,0:T(8...) while((s32[]{:T(128)}, bf16[8,240,128]{2,1,0:T(8,128)(2,1)}, ...), condition=%wide.region_12.13_spmd.clone, body=%wide.region_9.12_spmd.clone.sunk | while | flops 90404640 | bytes 3316033 | solution.py:74
  50.5 1.4 fusion.155
  53.2 1.4 fusion.155
  58.5 1.4 fusion.155
  63.9 1.4 fusion.155
  69.2 1.4 fusion.155
  71.9 3.7 %fusion.37 = bf16[1,240,2048]{2,1,0:T(8,128)(2,1)S(1)} fusion(bf16[1024,2048]{1,0:T(8,128)(2,1)} %param.23, bf16[8,240,128]{2,1,0:T(8,128)(2,1)} %get-tuple-element.134), kind=kOutput, calls=%fused_computation.57 | convolution fusion | flops 1007124480 | bytes 5668864 | tf_op jit(solution)/shard_map/dot_general | solution.py:107
  75.5 2.3 %fusion.38 = bf16[1,240,2048]{2,1,0:T(8,128)(2,1)S(1)} fusion(bf16[1024,2048]{1,0:T(8,128)(2,1)S(1)} %copy-done.1, bf16[8,240,128]{2,1,0:T(8,128)(2,1)} %get-tuple-element.135), kind=kOutput, calls=%fused_computation.58 | convolution fusion | flops 1007124480 | bytes 5668864 | tf_op jit(solution)/shard_map/dot_general | solution.py:107
  77.8 1.4 pad_maximum_fusion
  79.3 3.2 %collective-permute-start = (bf16[2,240,2048]{2,1,0:T(8,128)(2,1)}, bf16[2,240,2048]{2,1,0:T(8,128)(2,1)}, u32[]{:S(2)}, u32[]{:S(2)}) collective-permute-start(bf16[2,240,2048]{2,1,0:T(8,128)(2,1)} %pad_maximum_fusion), channel_id=1, source_target_pairs={{0,1},{1,0},{2,3},{3,2},{4,5},{5,4},{6,7},{7,6},{8,9},{9,8},{10,11... | collective-permute-start | bytes 5898248 | tf_op jit(solution)/shard_map/ppermute | solution.py:110
  86.5 20.7 %while.47 = (s32[]{:T(128)}, bf16[8,240,128]{2,1,0:T(8,128)(2,1)}, bf16[8,240,128]{2,1,0:T(8,128)(2,1)S(1)}, bf16[720,128]{1,0:T(8,128)(2,1)}, bf16[720,128]{1,0...) while((s32[]{:T(128)}, bf16[8,240,128]{2,1,0:T(8,128)(2,1)}, ...), condition=%wide.region_16.17_spmd.clone, body=%wide.region_13.16_spmd.clone.sunk | while | flops 90404640 | bytes 2580777 | solution.py:74
  110.0 8.7 %while.44 = (s32[]{:T(128)}, bf16[8,240,128]{2,1,0:T(8,128)(2,1)S(1)}, bf16[8,240,128]{2,1,0:T(8,128)(2,1)S(1)}, bf16[720,128]{1,0:T(8,128)(2,1)S(1)}, bf16[720,...) while((s32[]{:T(128)}, ...), condition=%wide.region_4.5_spmd.clone, body=%wide.region_1.4_spmd.clone.sunk | while | flops 90404640 | bytes 2626477 | solution.py:74
  119.7 4.0 %fusion.42 = bf16[240,2048]{1,0:T(8,128)(2,1)S(1)} fusion(bf16[2,240,2048]{2,1,0:T(8,128)(2,1)} %collective-permute-done, bf16[1024,2048]{1,0:T(8,128)(2,1)} %param.23, bf16[8,240,128]{2,1,0:T(8,128)(2,1)} %get-tuple-element.136), kind=kOutput, calls=%fused_computation.65 | convolution fusion | flops 1008107520 | bytes 6651904 | tf_op jit(solution)/shard_map/dot_general | solution.py:107
  126.5 22.1 %collective-permute-done.1 = bf16[240,2048]{1,0:T(8,128)(2,1)S(1)} collective-permute-done((bf16[240,2048]{1,0:T(8,128)(2,1)S(1)}, bf16[240,2048]{1,0:T(8,128)(2,1)S(1)}, u32[]{:S(2)}, u32[]{:S(2)}) %collective-permute-start.1) | collective-permute-done | bytes 983072 | tf_op jit(solution)/shard_map/ppermute | solution.py:112
  148.6 1.9 fusion.39
  152.7 1.7 collective-permute-done.2
  155.4 1.5 collective-permute-start.3
  157.2 15.1 %collective-permute-done.3 = bf16[2,75,2048]{2,0,1:T(2,128)(2,1)S(1)} collective-permute-done((bf16[2,75,2048]{2,0,1:T(2,128)(2,1)S(1)}, bf16[2,75,2048]{2,0,1:T(2,128)(2,1)S(1)}, u32[]{:S(2)}, u32[]{:S(2)}) %collective-permute-start.3) | collective-permute-done | bytes 614432 | tf_op jit(solution)/shard_map/ppermute | solution.py:138
  174.5 2.6 %convolution_multiply_fusion.4 = f32[2,75,2048]{2,1,0:T(8,128)S(1)} fusion(bf16[2,192,2048]{2,1,0:T(8,128)(2,1)S(1)} %copy-done, f32[2,75]{1,0:T(2,128)S(1)} %select_reduce_fusion, f32[2,75,192]{2,1,0:T(8,128)} %fusion.46, bf16[2,2,2048,192]{2,3,1,0:T(8,128)(2,1)} %param.25, bf16[2,75,2048]{2,1,0:T(8,128)(2,1)S(1)} %copy_add_fusion.2, ...), kind=kOutput, calls=%fused_computation.56 | convolution fusion | flops 236716800 | bytes 5767768 | tf_op jit(solution)/shard_map/ekf,efd->ekd/dot_general | solution.py:142
  179.4 2.5 %collective-permute-done.4 = f32[2,75,2048]{2,0,1:T(2,128)S(1)} collective-permute-done((f32[2,75,2048]{2,0,1:T(2,128)S(1)}, f32[2,75,2048]{2,0,1:T(2,128)S(1)}, u32[]{:S(2)}, u32[]{:S(2)}) %collective-permute-start.4) | collective-permute-done | bytes 1228832 | tf_op jit(solution)/shard_map/ppermute | solution.py:144
  184.6 15.3 %collective-permute-done.5 = bf16[2,75,2048]{2,0,1:T(2,128)(2,1)S(1)} collective-permute-done((bf16[2,75,2048]{2,0,1:T(2,128)(2,1)S(1)}, bf16[2,75,2048]{2,0,1:T(2,128)(2,1)S(1)}, u32[]{:S(2)}, u32[]{:S(2)}) %collective-permute-start.5) | collective-permute-done | bytes 614432 | tf_op jit(solution)/shard_map/ppermute | solution.py:145
  200.0 4.1 %fusion.36 = bf16[240,2048]{1,0:T(8,128)(2,1)} fusion(bf16[240,2048]{1,0:T(8,128)(2,1)S(1)} %copy-done.4, bf16[2,75,2048]{2,0,1:T(2,128)(2,1)S(1)} %collective-permute-done.5, f32[2,75,2048]{2,1,0:T(8,128)S(1)} %convolution_multiply_fusion.4, f32[2,75,2048]{2,0,1:T(2,128)S(1)} %collective-permute-done.4, pred[2,75,960]{2,1,0:T(8,128)(4,1)} %copy-done.17, ...), kind=kOutput, calls=%fused_computation.53 | convolution fusion | flops 887132160 | bytes 5079044 | tf_op jit(solution)/shard_map/ekt,ekd->td/dot_general | solution.py:148
  (262 shorter events, 97.1 us)
Async XLA Ops:
  0.0 174.5 %copy-start = (bf16[2,192,2048]{2,1,0:T(8,128)(2,1)S(1)}, bf16[2,192,2048]{2,1,0:T(8,128)(2,1)}, u32[]{:S(2)}) copy-start(bf16[2,192,2048]{2,1,0:T(8,128)(2,1)} %param.26) | copy-start | bytes 4718596
  4.6 6.7 %copy-start.18 = (s32[960]{0:T(1024)S(1)}, s32[960]{0:T(1024)}, u32[]{:S(2)}) copy-start(s32[960]{0:T(1024)} %param.27) | copy-start | bytes 11524
  9.6 4.6 %copy-start.5 = (f32[30,8,8,128]{3,1,2,0:T(8,128)S(1)}, f32[30,8,8,128]{3,1,2,0:T(8,128)}, u32[]{:S(2)}) copy-start(f32[30,8,8,128]{3,1,2,0:T(8,128)} %get-tuple-element.496) | copy-start | bytes 2949124
  9.6 4.8 %copy-start.26 = (f32[240]{0:T(256)S(1)}, f32[240]{0:T(256)}, u32[]{:S(2)}) copy-start(f32[240]{0:T(256)} %get-tuple-element.527) | copy-start | bytes 2884
  9.6 4.8 %copy-start.27 = (f32[240]{0:T(256)S(1)}, f32[240]{0:T(256)}, u32[]{:S(2)}) copy-start(f32[240]{0:T(256)} %get-tuple-element.528) | copy-start | bytes 2884
  9.6 4.8 %copy-start.34 = (f32[64]{0:T(128)S(1)}, f32[64]{0:T(128)}, u32[]{:S(2)}) copy-start(f32[64]{0:T(128)} %multiply_power_fusion) | copy-start | bytes 772
  17.7 6.0 %copy-start.31 = (s32[720]{0:T(1024)S(1)}, s32[720]{0:T(1024)}, u32[]{:S(2)}) copy-start(s32[720]{0:T(1024)} %get-tuple-element.821) | copy-start | bytes 8644
  17.7 6.0 %copy-start.32 = (s32[720]{0:T(1024)S(1)}, s32[720]{0:T(1024)}, u32[]{:S(2)}) copy-start(s32[720]{0:T(1024)} %get-tuple-element.824) | copy-start | bytes 8644
  17.7 6.0 %copy-start.38 = (s32[240]{0:T(256)S(1)}, s32[240]{0:T(256)}, u32[]{:S(2)}) copy-start(s32[240]{0:T(256)} %get-tuple-element.822) | copy-start | bytes 2884
  46.7 3.8 %copy-start.30 = (s32[720]{0:T(1024)S(1)}, s32[720]{0:T(1024)}, u32[]{:S(2)}) copy-start(s32[720]{0:T(1024)} %get-tuple-element.791) | copy-start | bytes 8644
  46.7 3.8 %copy-start.33 = (s32[720]{0:T(1024)S(1)}, s32[720]{0:T(1024)}, u32[]{:S(2)}) copy-start(s32[720]{0:T(1024)} %iota_add_fusion.1) | copy-start | bytes 8644
  46.8 3.8 %copy-start.37 = (s32[240]{0:T(256)S(1)}, s32[240]{0:T(256)}, u32[]{:S(2)}) copy-start(s32[240]{0:T(256)} %get-tuple-element.792) | copy-start | bytes 2884
  46.8 3.7 %copy-start.40 = (s32[240]{0:T(256)S(1)}, s32[240]{0:T(256)}, u32[]{:S(2)}) copy-start(s32[240]{0:T(256)} %iota_add_fusion.5) | copy-start | bytes 2884
  71.9 3.7 %copy-start.1 = (bf16[1024,2048]{1,0:T(8,128)(2,1)S(1)}, bf16[1024,2048]{1,0:T(8,128)(2,1)}, u32[]{:S(2)}) copy-start(bf16[1024,2048]{1,0:T(8,128)(2,1)} %param.23) | copy-start | bytes 12582916
  79.3 40.5 %collective-permute-start = (bf16[2,240,2048]{2,1,0:T(8,128)(2,1)}, bf16[2,240,2048]{2,1,0:T(8,128)(2,1)}, u32[]{:S(2)}, u32[]{:S(2)}) collective-permute-start(bf16[2,240,2048]{2,1,0:T(8,128)(2,1)} %pad_maximum_fusion), channel_id=1, source_target_pairs={{0,1},{1,0},{2,3},{3,2},{4,5},{5,4},{6,7},{7,6},{8,9},{9,8},{10,11... | collective-permute-start | bytes 5898248 | tf_op jit(solution)/shard_map/ppermute | solution.py:110
  84.0 2.6 %copy-start.20 = (bf16[720,128]{1,0:T(8,128)(2,1)S(1)}, bf16[720,128]{1,0:T(8,128)(2,1)}, u32[]{:S(2)}) copy-start(bf16[720,128]{1,0:T(8,128)(2,1)} %get-tuple-element.850) | copy-start | bytes 552964
  84.0 2.6 %copy-start.29 = (s32[720]{0:T(1024)S(1)}, s32[720]{0:T(1024)}, u32[]{:S(2)}) copy-start(s32[720]{0:T(1024)} %get-tuple-element.851) | copy-start | bytes 8644
  109.9 8.7 %copy-start.23 = (s32[960,8]{0,1:T(8,128)S(1)}, s32[960,8]{0,1:T(8,128)}, u32[]{:S(2)}) copy-start(s32[960,8]{0,1:T(8,128)} %param.28) | copy-start | bytes 92164
  119.7 5.5 %copy-start.2 = (bf16[1024,2048]{1,0:T(8,128)(2,1)S(1)}, bf16[1024,2048]{1,0:T(8,128)(2,1)}, u32[]{:S(2)}) copy-start(bf16[1024,2048]{1,0:T(8,128)(2,1)} %param.23) | copy-start | bytes 12582916
  123.7 24.9 %collective-permute-start.1 = (bf16[240,2048]{1,0:T(8,128)(2,1)S(1)}, bf16[240,2048]{1,0:T(8,128)(2,1)S(1)}, u32[]{:S(2)}, u32[]{:S(2)}) collective-permute-start(bf16[240,2048]{1,0:T(8,128)(2,1)S(1)} %fusion.42), channel_id=1, source_target_pairs={{0,2},{1,3},{2,0},{3,1},{4,6},{5,7},{6,4},{7,5},{8,10},{9,11},{10,... | collective-permute-start | bytes 2949128 | tf_op jit(solution)/shard_map/ppermute | solution.py:112
  125.2 25.3 %copy-start.17 = (pred[2,75,960]{2,1,0:T(8,128)(4,1)}, pred[2,75,960]{2,1,0:T(8,128)(4,1)S(1)}, u32[]{:S(2)}) copy-start(pred[2,75,960]{2,1,0:T(8,128)(4,1)S(1)} %fusion.59) | copy-start | bytes 432004
  125.2 23.4 %copy-start.6 = (bf16[240,2048]{1,0:T(8,128)(2,1)S(1)}, bf16[240,2048]{1,0:T(8,128)(2,1)}, u32[]{:S(2)}) copy-start(bf16[240,2048]{1,0:T(8,128)(2,1)} %param.22) | copy-start | bytes 2949124
  126.5 24.1 %copy-start.39 = (f32[2048]{0:T(1024)S(1)}, f32[2048]{0:T(1024)}, u32[]{:S(2)}) copy-start(f32[2048]{0:T(1024)} %param.24) | copy-start | bytes 24580
  150.5 4.3 %copy-start.3 = (bf16[240,2048]{1,0:T(8,128)(2,1)}, bf16[240,2048]{1,0:T(8,128)(2,1)S(1)}, u32[]{:S(2)}) copy-start(bf16[240,2048]{1,0:T(8,128)(2,1)S(1)} %get-tuple-element.486) | copy-start | bytes 2949124
  151.0 5.9 %copy-start.24 = (s32[960,8]{0,1:T(8,128)S(1)}, s32[960,8]{0,1:T(8,128)}, u32[]{:S(2)}) copy-start(s32[960,8]{0,1:T(8,128)} %param.28) | copy-start | bytes 92164
  151.0 5.9 %copy-start.25 = (f32[960,8]{0,1:T(8,128)S(1)}, f32[960,8]{0,1:T(8,128)}, u32[]{:S(2)}) copy-start(f32[960,8]{0,1:T(8,128)} %param.29) | copy-start | bytes 92164
  151.1 22.1 %copy-start.9 = (bf16[2,2,2048,192]{2,3,1,0:T(8,128)(2,1)S(1)}, bf16[2,2,2048,192]{2,3,1,0:T(8,128)(2,1)}, u32[]{:S(2)}) copy-start(bf16[2,2,2048,192]{2,3,1,0:T(8,128)(2,1)} %param.25) | copy-start | bytes 9437188
  151.7 2.6 %collective-permute-start.2 = (bf16[2,75,2048]{2,0,1:T(2,128)(2,1)S(1)}, bf16[2,75,2048]{2,0,1:T(2,128)(2,1)S(1)}, u32[]{:S(2)}, u32[]{:S(2)}) collective-permute-start(bf16[2,75,2048]{2,0,1:T(2,128)(2,1)S(1)} %copy.96), channel_id=1, source_target_pairs={{0,1},{1,0},{2,3},{3,2},{4,5},{5,4},{6,7},{7,6},{8,9},{9,8},{10,11... | collective-permute-start | bytes 1843208 | tf_op jit(solution)/shard_map/ppermute | solution.py:137
  155.4 16.9 %collective-permute-start.3 = (bf16[2,75,2048]{2,0,1:T(2,128)(2,1)S(1)}, bf16[2,75,2048]{2,0,1:T(2,128)(2,1)S(1)}, u32[]{:S(2)}, u32[]{:S(2)}) collective-permute-start(bf16[2,75,2048]{2,0,1:T(2,128)(2,1)S(1)} %copy.98), channel_id=1, source_target_pairs={{0,2},{1,3},{2,0},{3,1},{4,6},{5,7},{6,4},{7,5},{8,10},{9,11},{10,... | collective-permute-start | bytes 1843208 | tf_op jit(solution)/shard_map/ppermute | solution.py:138
  178.0 21.9 %copy-start.4 = (bf16[240,2048]{1,0:T(8,128)(2,1)S(1)}, bf16[240,2048]{1,0:T(8,128)(2,1)}, u32[]{:S(2)}) copy-start(bf16[240,2048]{1,0:T(8,128)(2,1)} %copy-done.3) | copy-start | bytes 2949124
  178.0 3.9 %collective-permute-start.4 = (f32[2,75,2048]{2,0,1:T(2,128)S(1)}, f32[2,75,2048]{2,0,1:T(2,128)S(1)}, u32[]{:S(2)}, u32[]{:S(2)}) collective-permute-start(f32[2,75,2048]{2,0,1:T(2,128)S(1)} %copy.102), channel_id=1, source_target_pairs={{0,1},{1,0},{2,3},{3,2},{4,5},{5,4},{6,7},{7,6},{8,9},{9,8},{10,11... | collective-permute-start | bytes 3686408 | tf_op jit(solution)/shard_map/ppermute | solution.py:144
  183.3 16.6 %collective-permute-start.5 = (bf16[2,75,2048]{2,0,1:T(2,128)(2,1)S(1)}, bf16[2,75,2048]{2,0,1:T(2,128)(2,1)S(1)}, u32[]{:S(2)}, u32[]{:S(2)}) collective-permute-start(bf16[2,75,2048]{2,0,1:T(2,128)(2,1)S(1)} %copy.104), channel_id=1, source_target_pairs={{0,2},{1,3},{2,0},{3,1},{4,6},{5,7},{6,4},{7,5},{8,10},{9,11},{10,... | collective-permute-start | bytes 1843208 | tf_op jit(solution)/shard_map/ppermute | solution.py:145
  (29 other events, 41.5 us)
